TPU v7x, 32 devices: a whole 2x2x4 slice. The times are simulated.
32 devices in a mesh: state: 2 (over x), member: 16 (over z, y, core).
Axes of the slice: x: 2, y: 2, z: 4, core: 2. Of those that a mesh axis runs over, the one named last changes fastest.
Arguments:
- state: float32 [2048, 1280], P('member', 'state'), may hold values from -6 to 6
- obs_values: float32 [2, 384], replicated, may hold values from -8 to 8
- noise_var: float32 [2, 384], replicated, may hold values from 0.3 to 3
- obs_rows: int32 [2, 384], replicated, may hold values from 0 to 639
- owner: int32 [2, 3], replicated, may hold values from 0 to 1
Outputs:
- analysis: float32 [2048, 1280], P('member', 'state')
All inputs are finite; a program needn't handle non-finite values.
Results may differ from a plain program's by a relative error of at most 0.0003.
Values sent between devices are 32-bit elements; how exact they have to be, the bound alone decides.
No kernel may reach another device: no remote copies, remote signals or barrier semaphores. Data moves between devices by JAX's collectives and lax.ppermute only.
A program may use at most 64 MiB of HBM per device.

v0:
```python
import jax
import jax.numpy as jnp
from jax import lax
from jax.sharding import PartitionSpec as P


def full_dot(left, right):
    return jnp.dot(left, right, precision=lax.Precision.HIGHEST, preferred_element_type=jnp.float32)


def tdot(left, right):
    return lax.dot_general(
        left, right, (((0,), (0,)), ((), ())),
        precision=lax.Precision.HIGHEST, preferred_element_type=jnp.float32,
    )


def _pow2(n):
    return n > 0 and (n & (n - 1)) == 0


def tree_sum(x, axis):
    n = lax.axis_size(axis)
    if n == 1:
        return x
    if not _pow2(n) or x.shape[0] % n != 0:
        return lax.psum(x, axis)
    me = lax.axis_index(axis)
    stages = []
    stride = 1
    while stride < n:
        radix = 4 if stride * 4 <= n else 2
        stages.append((stride, radix))
        stride *= radix
    cur = x
    for stride, radix in stages:
        digit = (me // stride) % radix
        h = cur.shape[0] // radix
        total = lax.dynamic_slice_in_dim(cur, digit * h, h, axis=0)
        for o in range(1, radix):
            perm = [(i, i + (((i // stride) % radix) ^ o) * stride - ((i // stride) % radix) * stride) for i in range(n)]
            away = lax.dynamic_slice_in_dim(cur, (digit ^ o) * h, h, axis=0)
            total = total + lax.ppermute(away, axis, perm)
        cur = total
    for stride, radix in reversed(stages):
        digit = (me // stride) % radix
        h = cur.shape[0]
        out = jnp.zeros((h * radix,) + cur.shape[1:], cur.dtype)
        out = lax.dynamic_update_slice_in_dim(out, cur, digit * h, axis=0)
        for o in range(1, radix):
            perm = [(i, i + (((i // stride) % radix) ^ o) * stride - ((i // stride) % radix) * stride) for i in range(n)]
            other = lax.ppermute(cur, axis, perm)
            out = lax.dynamic_update_slice_in_dim(out, other, (digit ^ o) * h, axis=0)
        cur = out
    return cur


def tree_sum_exact(x, axis):
    n = lax.axis_size(axis)
    if not _pow2(n):
        return lax.psum(x, axis)
    k = 1
    while k < n:
        perm = [(i, i ^ k) for i in range(n)]
        x = x + lax.ppermute(x, axis, perm)
        k *= 2
    return x


def block_solve(blk, right, size):
    nb = len(blk)
    eye = jnp.eye(size, dtype=right.dtype)
    rhs = [right[i * size:(i + 1) * size] for i in range(nb)]
    low = [[None] * nb for _ in range(nb)]
    inv = [None] * nb
    fwd = [None] * nb
    for k in range(nb):
        diag = lax.linalg.cholesky(blk[k][k], symmetrize_input=False)
        inv[k] = lax.linalg.triangular_solve(diag, eye, left_side=True, lower=True)
        fwd[k] = full_dot(inv[k], rhs[k])
        for i in range(k + 1, nb):
            low[i][k] = full_dot(blk[i][k], inv[k].T)
        for i in range(k + 1, nb):
            for j in range(k + 1, i + 1):
                blk[i][j] = blk[i][j] - full_dot(low[i][k], low[j][k].T)
            rhs[i] = rhs[i] - full_dot(low[i][k], fwd[k])
    out = [None] * nb
    for k in reversed(range(nb)):
        acc = fwd[k]
        for j in range(k + 1, nb):
            acc = acc - tdot(low[j][k], out[j])
        out[k] = tdot(inv[k], acc)
    return jnp.concatenate(out, axis=0)


def exchange(cands, owners_block):
    obs = cands.shape[1]
    tile = obs // owners_block.shape[0]
    own_each = jnp.repeat(owners_block, tile)
    mine = own_each[None, :] == lax.axis_index("state")
    return tree_sum_exact(jnp.where(mine, cands, 0.0), "state")


def analyse(current, observed, target, noise):
    m_loc = current.shape[0]
    n_member = lax.axis_size("member")
    count = m_loc * n_member
    me = lax.axis_index("member")
    n_rows = current.shape[1]
    obs = observed.shape[1]

    row_loc = jnp.mean(current, axis=0)
    obs_loc = jnp.mean(observed, axis=0)
    row_c = current - row_loc[None, :]
    obs_c = observed - obs_loc[None, :]
    gram_loc = tdot(obs_c, obs_c)
    cross_loc = tdot(obs_c, row_c)

    size = 128 if obs % 128 == 0 else obs
    nb = obs // size
    pairs = [(i, j) for i in range(nb) for j in range(i + 1)]
    width = -(-(obs + n_rows) // size) * size
    slots = jnp.zeros((n_member, width), jnp.float32)
    slots = lax.dynamic_update_slice(slots, jnp.concatenate([obs_loc, row_loc])[None, :], (me, 0))
    pieces = [gram_loc[i * size:(i + 1) * size, j * size:(j + 1) * size] for i, j in pairs]
    packed = jnp.concatenate(pieces + [slots.reshape(-1, size)], axis=0)
    packed = tree_sum(packed, "member")
    gram_blocks = packed[: len(pairs) * size]
    slots = packed[len(pairs) * size:].reshape(n_member, width)[:, : obs + n_rows]
    cross_loc, gram_blocks, slots = lax.optimization_barrier((cross_loc, gram_blocks, slots))
    cross_sum = tree_sum(cross_loc, "member")

    means = jnp.mean(slots, axis=0)
    dev = slots - means[None, :]
    obs_mean = means[:obs]
    dev_obs = dev[:, :obs]
    dev_row = dev[:, obs:]

    corr = m_loc * tdot(dev_obs, dev_obs)
    blk = [[None] * nb for _ in range(nb)]
    for p, (i, j) in enumerate(pairs):
        part = gram_blocks[p * size:(p + 1) * size] + corr[i * size:(i + 1) * size, j * size:(j + 1) * size]
        part = part / (count - 1.0)
        if i == j:
            part = 0.5 * (part + part.T) + jnp.diag(noise[i * size:(i + 1) * size])
        blk[i][j] = part
    obs_anom = observed - obs_mean[None, :]
    rhs = (target - obs_mean)[:, None] - 0.5 * obs_anom.T
    gain = block_solve(blk, rhs, size)

    cross = (cross_sum + m_loc * tdot(dev_obs, dev_row)) / (count - 1.0)
    return gain, cross


def shards(state, obs_values, noise_var, obs_rows, owner):
    num_blocks = obs_rows.shape[0]
    current = state
    cands = jnp.take(current, obs_rows[0], axis=1)
    for block in range(num_blocks):
        observed = exchange(cands, owner[block])
        gain, cross = analyse(current, observed, obs_values[block], noise_var[block])
        if block + 1 < num_blocks:
            rows = obs_rows[block + 1]
            cands = jnp.take(current, rows, axis=1) + full_dot(gain.T, jnp.take(cross, rows, axis=1))
        current = current + full_dot(gain.T, cross)
    return current


def solution(mesh):
    placed = (P("member", "state"), P(), P(), P(), P())
    return jax.shard_map(
        shards, mesh=mesh, in_specs=placed, out_specs=P("member", "state"), check_vma=False
    )
```

profile of v0, /device:TPU:0, one launch (start us, length us, event | category | flops | bytes accessed | tf_op | source)
XLA Modules:
  0.0 346.4 jit_solution(2836989206023019721)
XLA Ops:
  3.9 3.0 collective-permute-start
  8.4 3.4 collective-permute-done
  15.8 3.8 %collective-permute-done.2 = f32[224,128]{0,1:T(8,128)S(1)} collective-permute-done((f32[224,128]{0,1:T(8,128)S(1)}, f32[224,128]{0,1:T(8,128)S(1)}, u32[]{:S(2)}, u32[]{:S(2)}) %collective-permute-start.2) | collective-permute-done | bytes 114720 | tf_op jit(solution)/shard_map/ppermute | solution.py:43
  26.1 5.0 %collective-permute-done.5 = f32[56,128]{0,1:T(8,128)S(1)} collective-permute-done((f32[56,128]{0,1:T(8,128)S(1)}, f32[56,128]{0,1:T(8,128)S(1)}, u32[]{:S(2)}, u32[]{:S(2)}) %collective-permute-start.5) | collective-permute-done | bytes 28704 | tf_op jit(solution)/shard_map/ppermute | solution.py:43
  52.3 11.7 %custom-call.16 = f32[128,128]{1,0:T(8,128)S(1)} custom-call(f32[128,128]{1,0:T(8,128)S(1)} %copy.60), custom_call_target="Cholesky" | custom-call | tf_op jit(solution)/shard_map/cholesky/custom-call.1 | solution.py:78
  65.4 9.8 %custom-call.17 = f32[1,128,128]{1,2,0:T(8,128)S(1)} custom-call(f32[1,128,128]{2,1,0:T(8,128)S(1)} %fusion.41), custom_call_target="InvertDiagBlocksLowerTriangular" | custom-call | tf_op jit(solution)/shard_map/triangular_solve/custom-call.0 | solution.py:79
  77.7 11.7 %custom-call.18 = f32[128,128]{1,0:T(8,128)S(1)} custom-call(f32[128,128]{1,0:T(8,128)S(1)} %copy.66), custom_call_target="Cholesky" | custom-call | tf_op jit(solution)/shard_map/cholesky/custom-call.1 | solution.py:78
  91.2 9.8 %custom-call.19 = f32[1,128,128]{1,2,0:T(8,128)S(1)} custom-call(f32[1,128,128]{2,1,0:T(8,128)S(1)} %fusion.42), custom_call_target="InvertDiagBlocksLowerTriangular" | custom-call | tf_op jit(solution)/shard_map/triangular_solve/custom-call.0 | solution.py:79
  102.6 11.7 %custom-call.20 = f32[128,128]{1,0:T(8,128)S(1)} custom-call(f32[128,128]{1,0:T(8,128)S(1)} %copy.73), custom_call_target="Cholesky" | custom-call | tf_op jit(solution)/shard_map/cholesky/custom-call.1 | solution.py:78
  115.6 9.8 %custom-call.21 = f32[1,128,128]{1,2,0:T(8,128)S(1)} custom-call(f32[1,128,128]{2,1,0:T(8,128)S(1)} %fusion.43), custom_call_target="InvertDiagBlocksLowerTriangular" | custom-call | tf_op jit(solution)/shard_map/triangular_solve/custom-call.0 | solution.py:79
  129.5 6.8 %collective-permute-done.14 = f32[96,640]{1,0:T(8,128)S(1)} collective-permute-done((f32[96,640]{1,0:T(8,128)S(1)}, f32[96,640]{1,0:T(8,128)S(1)}, u32[]{:S(2)}, u32[]{:S(2)}) %collective-permute-start.14) | collective-permute-done | bytes 245792 | tf_op jit(solution)/shard_map/ppermute | solution.py:43
  136.4 3.5 %collective-permute-done.15 = f32[96,640]{1,0:T(8,128)S(1)} collective-permute-done((f32[96,640]{1,0:T(8,128)S(1)}, f32[96,640]{1,0:T(8,128)S(1)}, u32[]{:S(2)}, u32[]{:S(2)}) %collective-permute-start.15) | collective-permute-done | bytes 245792 | tf_op jit(solution)/shard_map/ppermute | solution.py:43
  144.7 4.8 %collective-permute-done.17 = f32[24,640]{1,0:T(8,128)S(1)} collective-permute-done((f32[24,640]{1,0:T(8,128)S(1)}, f32[24,640]{1,0:T(8,128)S(1)}, u32[]{:S(2)}, u32[]{:S(2)}) %collective-permute-start.17) | collective-permute-done | bytes 61472 | tf_op jit(solution)/shard_map/ppermute | solution.py:43
  154.4 3.6 %collective-permute-done.20 = f32[24,640]{1,0:T(8,128)S(1)} collective-permute-done((f32[24,640]{1,0:T(8,128)S(1)}, f32[24,640]{1,0:T(8,128)S(1)}, u32[]{:S(2)}, u32[]{:S(2)}) %collective-permute-start.20) | collective-permute-done | bytes 61472 | tf_op jit(solution)/shard_map/ppermute | solution.py:52
  161.1 6.5 %collective-permute-done.23 = f32[96,640]{1,0:T(8,128)S(1)} collective-permute-done((f32[96,640]{1,0:T(8,128)S(1)}, f32[96,640]{1,0:T(8,128)S(1)}, u32[]{:S(2)}, u32[]{:S(2)}) %collective-permute-start.23) | collective-permute-done | bytes 245792 | tf_op jit(solution)/shard_map/ppermute | solution.py:52
  167.7 4.2 %collective-permute-done.24 = f32[96,640]{1,0:T(8,128)S(1)} collective-permute-done((f32[96,640]{1,0:T(8,128)S(1)}, f32[96,640]{1,0:T(8,128)S(1)}, u32[]{:S(2)}, u32[]{:S(2)}) %collective-permute-start.24) | collective-permute-done | bytes 245792 | tf_op jit(solution)/shard_map/ppermute | solution.py:52
  178.5 5.7 %collective-permute-done.25 = f32[128,384]{1,0:T(8,128)S(1)} collective-permute-done((f32[128,384]{1,0:T(8,128)S(1)}, f32[128,384]{1,0:T(8,128)S(1)}, u32[]{:S(2)}, u32[]{:S(2)}) %collective-permute-start.25) | collective-permute-done | bytes 196640 | tf_op jit(solution)/shard_map/ppermute | solution.py:65
  187.4 4.6 %collective-permute-done.27 = f32[224,128]{0,1:T(8,128)S(1)} collective-permute-done((f32[224,128]{0,1:T(8,128)S(1)}, f32[224,128]{0,1:T(8,128)S(1)}, u32[]{:S(2)}, u32[]{:S(2)}) %collective-permute-start.27) | collective-permute-done | bytes 114720 | tf_op jit(solution)/shard_map/ppermute | solution.py:43
  198.4 5.1 %collective-permute-done.30 = f32[56,128]{0,1:T(8,128)S(1)} collective-permute-done((f32[56,128]{0,1:T(8,128)S(1)}, f32[56,128]{0,1:T(8,128)S(1)}, u32[]{:S(2)}, u32[]{:S(2)}) %collective-permute-start.30) | collective-permute-done | bytes 28704 | tf_op jit(solution)/shard_map/ppermute | solution.py:43
  209.6 3.0 collective-permute-done.33
  224.4 11.7 %custom-call.22 = f32[128,128]{1,0:T(8,128)S(1)} custom-call(f32[128,128]{1,0:T(8,128)S(1)} %fusion.75), custom_call_target="Cholesky" | custom-call | tf_op jit(solution)/shard_map/cholesky/custom-call.1 | solution.py:78
  237.5 9.8 %custom-call.23 = f32[1,128,128]{1,2,0:T(8,128)S(1)} custom-call(f32[1,128,128]{2,1,0:T(8,128)S(1)} %fusion.44), custom_call_target="InvertDiagBlocksLowerTriangular" | custom-call | tf_op jit(solution)/shard_map/triangular_solve/custom-call.0 | solution.py:79
  249.8 11.7 %custom-call.24 = f32[128,128]{1,0:T(8,128)S(1)} custom-call(f32[128,128]{1,0:T(8,128)S(1)} %convolution_subtract_fusion.9), custom_call_target="Cholesky" | custom-call | tf_op jit(solution)/shard_map/cholesky/custom-call.1 | solution.py:78
  263.1 9.8 %custom-call.25 = f32[1,128,128]{1,2,0:T(8,128)S(1)} custom-call(f32[1,128,128]{2,1,0:T(8,128)S(1)} %fusion.45), custom_call_target="InvertDiagBlocksLowerTriangular" | custom-call | tf_op jit(solution)/shard_map/triangular_solve/custom-call.0 | solution.py:79
  274.6 11.7 %custom-call.26 = f32[128,128]{1,0:T(8,128)S(1)} custom-call(f32[128,128]{1,0:T(8,128)S(1)} %convolution_subtract_fusion.5), custom_call_target="Cholesky" | custom-call | tf_op jit(solution)/shard_map/cholesky/custom-call.1 | solution.py:78
  287.6 9.8 %custom-call.27 = f32[1,128,128]{1,2,0:T(8,128)S(1)} custom-call(f32[1,128,128]{2,1,0:T(8,128)S(1)} %fusion.46), custom_call_target="InvertDiagBlocksLowerTriangular" | custom-call | tf_op jit(solution)/shard_map/triangular_solve/custom-call.0 | solution.py:79
  301.6 6.8 %collective-permute-done.39 = f32[96,640]{1,0:T(8,128)S(1)} collective-permute-done((f32[96,640]{1,0:T(8,128)S(1)}, f32[96,640]{1,0:T(8,128)S(1)}, u32[]{:S(2)}, u32[]{:S(2)}) %collective-permute-start.39) | collective-permute-done | bytes 245792 | tf_op jit(solution)/shard_map/ppermute | solution.py:43
  308.4 3.5 %collective-permute-done.40 = f32[96,640]{1,0:T(8,128)S(1)} collective-permute-done((f32[96,640]{1,0:T(8,128)S(1)}, f32[96,640]{1,0:T(8,128)S(1)}, u32[]{:S(2)}, u32[]{:S(2)}) %collective-permute-start.40) | collective-permute-done | bytes 245792 | tf_op jit(solution)/shard_map/ppermute | solution.py:43
  316.7 4.4 %collective-permute-done.42 = f32[24,640]{1,0:T(8,128)S(1)} collective-permute-done((f32[24,640]{1,0:T(8,128)S(1)}, f32[24,640]{1,0:T(8,128)S(1)}, u32[]{:S(2)}, u32[]{:S(2)}) %collective-permute-start.42) | collective-permute-done | bytes 61472 | tf_op jit(solution)/shard_map/ppermute | solution.py:43
  325.9 3.4 collective-permute-done.45
  332.6 6.5 %collective-permute-done.48 = f32[96,640]{1,0:T(8,128)S(1)} collective-permute-done((f32[96,640]{1,0:T(8,128)S(1)}, f32[96,640]{1,0:T(8,128)S(1)}, u32[]{:S(2)}, u32[]{:S(2)}) %collective-permute-start.48) | collective-permute-done | bytes 245792 | tf_op jit(solution)/shard_map/ppermute | solution.py:52
  339.2 4.2 %collective-permute-done.49 = f32[96,640]{1,0:T(8,128)S(1)} collective-permute-done((f32[96,640]{1,0:T(8,128)S(1)}, f32[96,640]{1,0:T(8,128)S(1)}, u32[]{:S(2)}, u32[]{:S(2)}) %collective-permute-start.49) | collective-permute-done | bytes 245792 | tf_op jit(solution)/shard_map/ppermute | solution.py:52
  (304 shorter events, 123.4 us)
Async XLA Ops:
  3.9 7.9 %collective-permute-start = (f32[128,384]{1,0:T(8,128)S(1)}, f32[128,384]{1,0:T(8,128)S(1)}, u32[]{:S(2)}, u32[]{:S(2)}) collective-permute-start(f32[128,384]{1,0:T(8,128)S(1)} %bitcast_select_fusion), channel_id=1, source_target_pairs={{0,16},{16,0},{1,17},{17,1},{2,18},{18,2},{3,19},{19,3},{4,20},{20... | collective-permute-start | bytes 589832 | tf_op jit(solution)/shard_map/ppermute | solution.py:65
  13.2 6.4 %collective-permute-start.2 = (f32[224,128]{0,1:T(8,128)S(1)}, f32[224,128]{0,1:T(8,128)S(1)}, u32[]{:S(2)}, u32[]{:S(2)}) collective-permute-start(f32[224,128]{0,1:T(8,128)S(1)} %get-tuple-element.49), channel_id=1, source_target_pairs={{0,2},{1,3},{2,0},{3,1},{4,6},{5,7},{6,4},{7,5},{8,10},{9,11},{10,... | collective-permute-start | bytes 344072 | tf_op jit(solution)/shard_map/ppermute | solution.py:43
  15.0 6.4 %collective-permute-start.3 = (f32[224,128]{0,1:T(8,128)S(1)}, f32[224,128]{0,1:T(8,128)S(1)}, u32[]{:S(2)}, u32[]{:S(2)}) collective-permute-start(f32[224,128]{0,1:T(8,128)S(1)} %get-tuple-element.48), channel_id=1, source_target_pairs={{0,3},{1,2},{2,1},{3,0},{4,7},{5,6},{6,5},{7,4},{8,11},{9,10},{10,... | collective-permute-start | bytes 344072 | tf_op jit(solution)/shard_map/ppermute | solution.py:43
  23.5 7.6 %collective-permute-start.5 = (f32[56,128]{0,1:T(8,128)S(1)}, f32[56,128]{0,1:T(8,128)S(1)}, u32[]{:S(2)}, u32[]{:S(2)}) collective-permute-start(f32[56,128]{0,1:T(8,128)S(1)} %get-tuple-element.61), channel_id=1, source_target_pairs={{0,8},{1,9},{2,10},{3,11},{4,12},{5,13},{6,14},{7,15},{8,0},{9,1},... | collective-permute-start | bytes 86024 | tf_op jit(solution)/shard_map/ppermute | solution.py:43
  32.2 6.6 %collective-permute-start.7 = (f32[56,128]{0,1:T(8,128)S(1)}, f32[56,128]{0,1:T(8,128)S(1)}, u32[]{:S(2)}, u32[]{:S(2)}) collective-permute-start(f32[56,128]{0,1:T(8,128)S(1)} %add_add_fusion.5), channel_id=1, source_target_pairs={{0,4},{1,5},{2,6},{3,7},{4,0},{5,1},{6,2},{7,3},{8,12},{9,13},{10,... | collective-permute-start | bytes 86024 | tf_op jit(solution)/shard_map/ppermute | solution.py:52
  33.5 6.8 %collective-permute-start.8 = (f32[56,128]{0,1:T(8,128)S(1)}, f32[56,128]{0,1:T(8,128)S(1)}, u32[]{:S(2)}, u32[]{:S(2)}) collective-permute-start(f32[56,128]{0,1:T(8,128)S(1)} %add_add_fusion.5), channel_id=1, source_target_pairs={{0,8},{1,9},{2,10},{3,11},{4,12},{5,13},{6,14},{7,15},{8,0},{9,1},... | collective-permute-start | bytes 86024 | tf_op jit(solution)/shard_map/ppermute | solution.py:52
  35.2 6.2 %collective-permute-start.9 = (f32[56,128]{0,1:T(8,128)S(1)}, f32[56,128]{0,1:T(8,128)S(1)}, u32[]{:S(2)}, u32[]{:S(2)}) collective-permute-start(f32[56,128]{0,1:T(8,128)S(1)} %add_add_fusion.5), channel_id=1, source_target_pairs={{0,12},{1,13},{2,14},{3,15},{4,8},{5,9},{6,10},{7,11},{8,4},{9,5},... | collective-permute-start | bytes 86024 | tf_op jit(solution)/shard_map/ppermute | solution.py:52
  42.0 6.4 %collective-permute-start.11 = (f32[224,128]{0,1:T(8,128)S(1)}, f32[224,128]{0,1:T(8,128)S(1)}, u32[]{:S(2)}, u32[]{:S(2)}) collective-permute-start(f32[224,128]{0,1:T(8,128)S(1)} %dynamic_update_slice.106), channel_id=1, source_target_pairs={{0,2},{1,3},{2,0},{3,1},{4,6},{5,7},{6,4},{7,5},{8,10},{9,11},{10,... | collective-permute-start | bytes 344072 | tf_op jit(solution)/shard_map/ppermute | solution.py:52
  43.6 6.6 %collective-permute-start.12 = (f32[224,128]{0,1:T(8,128)S(1)}, f32[224,128]{0,1:T(8,128)S(1)}, u32[]{:S(2)}, u32[]{:S(2)}) collective-permute-start(f32[224,128]{0,1:T(8,128)S(1)} %dynamic_update_slice.106), channel_id=1, source_target_pairs={{0,3},{1,2},{2,1},{3,0},{4,7},{5,6},{6,5},{7,4},{8,11},{9,10},{10,... | collective-permute-start | bytes 344072 | tf_op jit(solution)/shard_map/ppermute | solution.py:52
  127.5 8.8 %collective-permute-start.14 = (f32[96,640]{1,0:T(8,128)S(1)}, f32[96,640]{1,0:T(8,128)S(1)}, u32[]{:S(2)}, u32[]{:S(2)}) collective-permute-start(f32[96,640]{1,0:T(8,128)S(1)} %get-tuple-element.43), channel_id=1, source_target_pairs={{0,2},{1,3},{2,0},{3,1},{4,6},{5,7},{6,4},{7,5},{8,10},{9,11},{10,... | collective-permute-start | bytes 737288 | tf_op jit(solution)/shard_map/ppermute | solution.py:43
  128.8 11.0 %collective-permute-start.15 = (f32[96,640]{1,0:T(8,128)S(1)}, f32[96,640]{1,0:T(8,128)S(1)}, u32[]{:S(2)}, u32[]{:S(2)}) collective-permute-start(f32[96,640]{1,0:T(8,128)S(1)} %get-tuple-element.42), channel_id=1, source_target_pairs={{0,3},{1,2},{2,1},{3,0},{4,7},{5,6},{6,5},{7,4},{8,11},{9,10},{10,... | collective-permute-start | bytes 737288 | tf_op jit(solution)/shard_map/ppermute | solution.py:43
  141.2 8.3 %collective-permute-start.17 = (f32[24,640]{1,0:T(8,128)S(1)}, f32[24,640]{1,0:T(8,128)S(1)}, u32[]{:S(2)}, u32[]{:S(2)}) collective-permute-start(f32[24,640]{1,0:T(8,128)S(1)} %get-tuple-element.55), channel_id=1, source_target_pairs={{0,8},{1,9},{2,10},{3,11},{4,12},{5,13},{6,14},{7,15},{8,0},{9,1},... | collective-permute-start | bytes 184328 | tf_op jit(solution)/shard_map/ppermute | solution.py:43
  143.1 6.4 %collective-permute-start.18 = (f32[24,640]{1,0:T(8,128)S(1)}, f32[24,640]{1,0:T(8,128)S(1)}, u32[]{:S(2)}, u32[]{:S(2)}) collective-permute-start(f32[24,640]{1,0:T(8,128)S(1)} %get-tuple-element.54), channel_id=1, source_target_pairs={{0,12},{1,13},{2,14},{3,15},{4,8},{5,9},{6,10},{7,11},{8,4},{9,5},... | collective-permute-start | bytes 184328 | tf_op jit(solution)/shard_map/ppermute | solution.py:43
  151.3 6.6 %collective-permute-start.20 = (f32[24,640]{1,0:T(8,128)S(1)}, f32[24,640]{1,0:T(8,128)S(1)}, u32[]{:S(2)}, u32[]{:S(2)}) collective-permute-start(f32[24,640]{1,0:T(8,128)S(1)} %get-tuple-element.29), channel_id=1, source_target_pairs={{0,8},{1,9},{2,10},{3,11},{4,12},{5,13},{6,14},{7,15},{8,0},{9,1},... | collective-permute-start | bytes 184328 | tf_op jit(solution)/shard_map/ppermute | solution.py:52
  158.8 8.9 %collective-permute-start.23 = (f32[96,640]{1,0:T(8,128)S(1)}, f32[96,640]{1,0:T(8,128)S(1)}, u32[]{:S(2)}, u32[]{:S(2)}) collective-permute-start(f32[96,640]{1,0:T(8,128)S(1)} %constant_dynamic-update-slice_fusion.14), channel_id=1, source_target_pairs={{0,2},{1,3},{2,0},{3,1},{4,6},{5,7},{6,4},{7,5},{8,10},{9,11},{10,... | collective-permute-start | bytes 737288 | tf_op jit(solution)/shard_map/ppermute | solution.py:52
  160.9 11.0 %collective-permute-start.24 = (f32[96,640]{1,0:T(8,128)S(1)}, f32[96,640]{1,0:T(8,128)S(1)}, u32[]{:S(2)}, u32[]{:S(2)}) collective-permute-start(f32[96,640]{1,0:T(8,128)S(1)} %constant_dynamic-update-slice_fusion.14), channel_id=1, source_target_pairs={{0,3},{1,2},{2,1},{3,0},{4,7},{5,6},{6,5},{7,4},{8,11},{9,10},{10,... | collective-permute-start | bytes 737288 | tf_op jit(solution)/shard_map/ppermute | solution.py:52
  176.9 7.2 %collective-permute-start.25 = (f32[128,384]{1,0:T(8,128)S(1)}, f32[128,384]{1,0:T(8,128)S(1)}, u32[]{:S(2)}, u32[]{:S(2)}) collective-permute-start(f32[128,384]{1,0:T(8,128)S(1)} %fusion.4), channel_id=1, source_target_pairs={{0,16},{16,0},{1,17},{17,1},{2,18},{18,2},{3,19},{19,3},{4,20},{20... | collective-permute-start | bytes 589832 | tf_op jit(solution)/shard_map/ppermute | solution.py:65
  185.5 6.4 %collective-permute-start.27 = (f32[224,128]{0,1:T(8,128)S(1)}, f32[224,128]{0,1:T(8,128)S(1)}, u32[]{:S(2)}, u32[]{:S(2)}) collective-permute-start(f32[224,128]{0,1:T(8,128)S(1)} %get-tuple-element.46), channel_id=1, source_target_pairs={{0,2},{1,3},{2,0},{3,1},{4,6},{5,7},{6,4},{7,5},{8,10},{9,11},{10,... | collective-permute-start | bytes 344072 | tf_op jit(solution)/shard_map/ppermute | solution.py:43
  187.3 6.4 %collective-permute-start.28 = (f32[224,128]{0,1:T(8,128)S(1)}, f32[224,128]{0,1:T(8,128)S(1)}, u32[]{:S(2)}, u32[]{:S(2)}) collective-permute-start(f32[224,128]{0,1:T(8,128)S(1)} %get-tuple-element.45), channel_id=1, source_target_pairs={{0,3},{1,2},{2,1},{3,0},{4,7},{5,6},{6,5},{7,4},{8,11},{9,10},{10,... | collective-permute-start | bytes 344072 | tf_op jit(solution)/shard_map/ppermute | solution.py:43
  195.1 8.4 %collective-permute-start.30 = (f32[56,128]{0,1:T(8,128)S(1)}, f32[56,128]{0,1:T(8,128)S(1)}, u32[]{:S(2)}, u32[]{:S(2)}) collective-permute-start(f32[56,128]{0,1:T(8,128)S(1)} %get-tuple-element.58), channel_id=1, source_target_pairs={{0,8},{1,9},{2,10},{3,11},{4,12},{5,13},{6,14},{7,15},{8,0},{9,1},... | collective-permute-start | bytes 86024 | tf_op jit(solution)/shard_map/ppermute | solution.py:43
  196.3 7.2 %collective-permute-start.31 = (f32[56,128]{0,1:T(8,128)S(1)}, f32[56,128]{0,1:T(8,128)S(1)}, u32[]{:S(2)}, u32[]{:S(2)}) collective-permute-start(f32[56,128]{0,1:T(8,128)S(1)} %get-tuple-element.57), channel_id=1, source_target_pairs={{0,12},{1,13},{2,14},{3,15},{4,8},{5,9},{6,10},{7,11},{8,4},{9,5},... | collective-permute-start | bytes 86024 | tf_op jit(solution)/shard_map/ppermute | solution.py:43
  205.1 7.6 %collective-permute-start.33 = (f32[56,128]{0,1:T(8,128)S(1)}, f32[56,128]{0,1:T(8,128)S(1)}, u32[]{:S(2)}, u32[]{:S(2)}) collective-permute-start(f32[56,128]{0,1:T(8,128)S(1)} %add_add_fusion.4), channel_id=1, source_target_pairs={{0,8},{1,9},{2,10},{3,11},{4,12},{5,13},{6,14},{7,15},{8,0},{9,1},... | collective-permute-start | bytes 86024 | tf_op jit(solution)/shard_map/ppermute | solution.py:52
  206.1 7.4 %collective-permute-start.34 = (f32[56,128]{0,1:T(8,128)S(1)}, f32[56,128]{0,1:T(8,128)S(1)}, u32[]{:S(2)}, u32[]{:S(2)}) collective-permute-start(f32[56,128]{0,1:T(8,128)S(1)} %add_add_fusion.4), channel_id=1, source_target_pairs={{0,12},{1,13},{2,14},{3,15},{4,8},{5,9},{6,10},{7,11},{8,4},{9,5},... | collective-permute-start | bytes 86024 | tf_op jit(solution)/shard_map/ppermute | solution.py:52
  214.1 6.4 %collective-permute-start.36 = (f32[224,128]{0,1:T(8,128)S(1)}, f32[224,128]{0,1:T(8,128)S(1)}, u32[]{:S(2)}, u32[]{:S(2)}) collective-permute-start(f32[224,128]{0,1:T(8,128)S(1)} %dynamic_update_slice.123), channel_id=1, source_target_pairs={{0,2},{1,3},{2,0},{3,1},{4,6},{5,7},{6,4},{7,5},{8,10},{9,11},{10,... | collective-permute-start | bytes 344072 | tf_op jit(solution)/shard_map/ppermute | solution.py:52
  215.5 6.8 %collective-permute-start.37 = (f32[224,128]{0,1:T(8,128)S(1)}, f32[224,128]{0,1:T(8,128)S(1)}, u32[]{:S(2)}, u32[]{:S(2)}) collective-permute-start(f32[224,128]{0,1:T(8,128)S(1)} %dynamic_update_slice.123), channel_id=1, source_target_pairs={{0,3},{1,2},{2,1},{3,0},{4,7},{5,6},{6,5},{7,4},{8,11},{9,10},{10,... | collective-permute-start | bytes 344072 | tf_op jit(solution)/shard_map/ppermute | solution.py:52
  299.5 8.8 %collective-permute-start.39 = (f32[96,640]{1,0:T(8,128)S(1)}, f32[96,640]{1,0:T(8,128)S(1)}, u32[]{:S(2)}, u32[]{:S(2)}) collective-permute-start(f32[96,640]{1,0:T(8,128)S(1)} %get-tuple-element.37), channel_id=1, source_target_pairs={{0,2},{1,3},{2,0},{3,1},{4,6},{5,7},{6,4},{7,5},{8,10},{9,11},{10,... | collective-permute-start | bytes 737288 | tf_op jit(solution)/shard_map/ppermute | solution.py:43
  300.6 11.3 %collective-permute-start.40 = (f32[96,640]{1,0:T(8,128)S(1)}, f32[96,640]{1,0:T(8,128)S(1)}, u32[]{:S(2)}, u32[]{:S(2)}) collective-permute-start(f32[96,640]{1,0:T(8,128)S(1)} %get-tuple-element.36), channel_id=1, source_target_pairs={{0,3},{1,2},{2,1},{3,0},{4,7},{5,6},{6,5},{7,4},{8,11},{9,10},{10,... | collective-permute-start | bytes 737288 | tf_op jit(solution)/shard_map/ppermute | solution.py:43
  312.7 8.4 %collective-permute-start.42 = (f32[24,640]{1,0:T(8,128)S(1)}, f32[24,640]{1,0:T(8,128)S(1)}, u32[]{:S(2)}, u32[]{:S(2)}) collective-permute-start(f32[24,640]{1,0:T(8,128)S(1)} %get-tuple-element.52), channel_id=1, source_target_pairs={{0,8},{1,9},{2,10},{3,11},{4,12},{5,13},{6,14},{7,15},{8,0},{9,1},... | collective-permute-start | bytes 184328 | tf_op jit(solution)/shard_map/ppermute | solution.py:43
  314.6 6.5 %collective-permute-start.43 = (f32[24,640]{1,0:T(8,128)S(1)}, f32[24,640]{1,0:T(8,128)S(1)}, u32[]{:S(2)}, u32[]{:S(2)}) collective-permute-start(f32[24,640]{1,0:T(8,128)S(1)} %get-tuple-element.51), channel_id=1, source_target_pairs={{0,12},{1,13},{2,14},{3,15},{4,8},{5,9},{6,10},{7,11},{8,4},{9,5},... | collective-permute-start | bytes 184328 | tf_op jit(solution)/shard_map/ppermute | solution.py:43
  322.8 6.5 %collective-permute-start.45 = (f32[24,640]{1,0:T(8,128)S(1)}, f32[24,640]{1,0:T(8,128)S(1)}, u32[]{:S(2)}, u32[]{:S(2)}) collective-permute-start(f32[24,640]{1,0:T(8,128)S(1)} %get-tuple-element.25), channel_id=1, source_target_pairs={{0,8},{1,9},{2,10},{3,11},{4,12},{5,13},{6,14},{7,15},{8,0},{9,1},... | collective-permute-start | bytes 184328 | tf_op jit(solution)/shard_map/ppermute | solution.py:52
  330.3 8.9 %collective-permute-start.48 = (f32[96,640]{1,0:T(8,128)S(1)}, f32[96,640]{1,0:T(8,128)S(1)}, u32[]{:S(2)}, u32[]{:S(2)}) collective-permute-start(f32[96,640]{1,0:T(8,128)S(1)} %constant_dynamic-update-slice_fusion.6), channel_id=1, source_target_pairs={{0,2},{1,3},{2,0},{3,1},{4,6},{5,7},{6,4},{7,5},{8,10},{9,11},{10,... | collective-permute-start | bytes 737288 | tf_op jit(solution)/shard_map/ppermute | solution.py:52
  332.1 11.2 %collective-permute-start.49 = (f32[96,640]{1,0:T(8,128)S(1)}, f32[96,640]{1,0:T(8,128)S(1)}, u32[]{:S(2)}, u32[]{:S(2)}) collective-permute-start(f32[96,640]{1,0:T(8,128)S(1)} %constant_dynamic-update-slice_fusion.6), channel_id=1, source_target_pairs={{0,3},{1,2},{2,1},{3,0},{4,7},{5,6},{6,5},{7,4},{8,11},{9,10},{10,... | collective-permute-start | bytes 737288 | tf_op jit(solution)/shard_map/ppermute | solution.py:52
  (23 other events, 81.2 us)
where the time goes:
time: 352 us; the launch traced here: 346 us
  other arithmetic  139 us (39%)
  waiting for transfers between devices  99.1 us (28%)
  starting transfers between devices  56.6 us (16%)
  local copies, waits for them, and re-layouts  27.3 us (8%)
  matrix products  22.5 us (6%)
    another operation x19, other arithmetic, block_solve(): diag = lax.linalg.cholesky(blk[k][k], symmetrize_input=False)  75 us
    another operation x12, other arithmetic, block_solve(): inv[k] = lax.linalg.triangular_solve(diag, eye, left_side=True, lower=True)  62.8 us
    ppermute x24, waiting for transfers between devices, tree_sum(): total = total + lax.ppermute(away, axis, perm)  52.8 us
    ppermute x24, waiting for transfers between devices, tree_sum(): other = lax.ppermute(cur, axis, perm)  37.2 us
    ppermute x24, starting transfers between devices, tree_sum(): total = total + lax.ppermute(away, axis, perm)  26.3 us
    ppermute x24, starting transfers between devices, tree_sum(): other = lax.ppermute(cur, axis, perm)  25.8 us
    dynamic_update_slice x24, local copies, waits for them, and re-layouts, tree_sum(): out = lax.dynamic_update_slice_in_dim(out, other, (digit ^ o) * h, axis=0)  11.6 us
    dot_general x29, matrix products, full_dot(): jnp.dot(left, right, precision=lax.Precision.HIGHEST, preferred_element_t...  10.6 us
  transfers between devices with their start and end apart: 50, of which 30 were waited for; matrix products, arithmetic and copies ran while one was open for 5% of the time, Pallas kernels for 0%

commit v1 on v0

--- a/solution.py
+++ b/solution.py
@@ -26,32 +26,23 @@
     if not _pow2(n) or x.shape[0] % n != 0:
         return lax.psum(x, axis)
     me = lax.axis_index(axis)
-    stages = []
-    stride = 1
-    while stride < n:
-        radix = 4 if stride * 4 <= n else 2
-        stages.append((stride, radix))
-        stride *= radix
     cur = x
-    for stride, radix in stages:
-        digit = (me // stride) % radix
-        h = cur.shape[0] // radix
-        total = lax.dynamic_slice_in_dim(cur, digit * h, h, axis=0)
-        for o in range(1, radix):
-            perm = [(i, i + (((i // stride) % radix) ^ o) * stride - ((i // stride) % radix) * stride) for i in range(n)]
-            away = lax.dynamic_slice_in_dim(cur, (digit ^ o) * h, h, axis=0)
-            total = total + lax.ppermute(away, axis, perm)
-        cur = total
-    for stride, radix in reversed(stages):
-        digit = (me // stride) % radix
-        h = cur.shape[0]
-        out = jnp.zeros((h * radix,) + cur.shape[1:], cur.dtype)
-        out = lax.dynamic_update_slice_in_dim(out, cur, digit * h, axis=0)
-        for o in range(1, radix):
-            perm = [(i, i + (((i // stride) % radix) ^ o) * stride - ((i // stride) % radix) * stride) for i in range(n)]
-            other = lax.ppermute(cur, axis, perm)
-            out = lax.dynamic_update_slice_in_dim(out, other, (digit ^ o) * h, axis=0)
-        cur = out
+    k = 1
+    while k < n:
+        perm = [(i, i ^ k) for i in range(n)]
+        h = cur.shape[0] // 2
+        bit = (me // k) % 2
+        keep = lax.dynamic_slice_in_dim(cur, bit * h, h, axis=0)
+        away = lax.dynamic_slice_in_dim(cur, (1 - bit) * h, h, axis=0)
+        cur = keep + lax.ppermute(away, axis, perm)
+        k *= 2
+    k = n // 2
+    while k >= 1:
+        perm = [(i, i ^ k) for i in range(n)]
+        bit = (me // k) % 2
+        other = lax.ppermute(cur, axis, perm)
+        cur = jnp.where(bit == 0, jnp.concatenate([cur, other]), jnp.concatenate([other, cur]))
+        k //= 2
     return cur
 
 
@@ -152,7 +143,7 @@
     return gain, cross
 
 
-def shards(state, obs_values, noise_var, obs_rows, owner):
+def serial(state, obs_values, noise_var, obs_rows, owner):
     num_blocks = obs_rows.shape[0]
     current = state
     cands = jnp.take(current, obs_rows[0], axis=1)
@@ -166,6 +157,112 @@
     return current
 
 
+def lower_blocks(cov, size, noise, count):
+    nb = cov.shape[0] // size
+    blk = [[None] * nb for _ in range(nb)]
+    for i in range(nb):
+        for j in range(i + 1):
+            part = cov[i * size:(i + 1) * size, j * size:(j + 1) * size] / (count - 1.0)
+            if i == j:
+                part = 0.5 * (part + part.T) + jnp.diag(noise[i * size:(i + 1) * size])
+            blk[i][j] = part
+    return blk
+
+
+def two_blocks(state, obs_values, noise_var, obs_rows, owner):
+    m_loc, n_rows = state.shape
+    n_member = lax.axis_size("member")
+    count = m_loc * n_member
+    me = lax.axis_index("member")
+    obs = obs_rows.shape[1]
+    size = 128 if obs % 128 == 0 else obs
+
+    cands = jnp.concatenate([jnp.take(state, obs_rows[0], axis=1), jnp.take(state, obs_rows[1], axis=1)], axis=1)
+    tile = obs // owner.shape[1]
+    own_each = jnp.concatenate([jnp.repeat(owner[0], tile), jnp.repeat(owner[1], tile)])
+    mine = own_each[None, :] == lax.axis_index("state")
+    both = tree_sum_exact(jnp.where(mine, cands, 0.0), "state")
+
+    row_loc = jnp.mean(state, axis=0)
+    both_loc = jnp.mean(both, axis=0)
+    row_c = state - row_loc[None, :]
+    both_c = both - both_loc[None, :]
+    gram_loc = tdot(both_c, both_c)
+    cross_loc = tdot(both_c[:, :obs], row_c)
+
+    wide = 2 * obs
+    nbw = wide // size
+    pairs = [(i, j) for i in range(nbw) for j in range(i + 1)]
+    width = -(-(wide + n_rows) // size) * size
+    slots = jnp.zeros((n_member, width), jnp.float32)
+    slots = lax.dynamic_update_slice(slots, jnp.concatenate([both_loc, row_loc])[None, :], (me, 0))
+    pieces = [gram_loc[i * size:(i + 1) * size, j * size:(j + 1) * size] for i, j in pairs]
+    packed = jnp.concatenate(pieces + [slots.reshape(-1, size)], axis=0)
+    packed = tree_sum(packed, "member")
+    gram_blocks = packed[: len(pairs) * size]
+    slots = packed[len(pairs) * size:].reshape(n_member, width)[:, : wide + n_rows]
+    cross_loc, gram_blocks, slots = lax.optimization_barrier((cross_loc, gram_blocks, slots))
+    cross_sum = tree_sum(cross_loc, "member")
+
+    means = jnp.mean(slots, axis=0)
+    dev = slots - means[None, :]
+    dev_both = dev[:, :wide]
+    dev_row = dev[:, wide:]
+    corr = m_loc * tdot(dev_both, dev_both)
+    rows_of = []
+    for i in range(nbw):
+        cols = []
+        for j in range(nbw):
+            if j <= i:
+                p = pairs.index((i, j))
+                part = gram_blocks[p * size:(p + 1) * size]
+            else:
+                p = pairs.index((j, i))
+                part = gram_blocks[p * size:(p + 1) * size].T
+            cols.append(part)
+        rows_of.append(jnp.concatenate(cols, axis=1))
+    moments = jnp.concatenate(rows_of, axis=0) + corr
+    gram0 = moments[:obs, :obs]
+    zs = moments[:obs, obs:]
+    k1 = moments[obs:, obs:]
+
+    mean0 = means[:obs]
+    mean1 = means[obs:wide]
+    row_mean0 = means[wide:]
+    x0 = both[:, :obs]
+    x1 = both[:, obs:]
+
+    anom0 = x0 - mean0[None, :]
+    d0 = obs_values[0] - mean0
+    zp = zs / (count - 1.0)
+    rhs0 = jnp.concatenate([d0[:, None] - 0.5 * anom0.T, d0[:, None], zp], axis=1)
+    sol0 = block_solve(lower_blocks(gram0, size, noise_var[0], count), rhs0, size)
+    gain0 = sol0[:, :m_loc]
+    w0 = sol0[:, m_loc]
+    wmat = sol0[:, m_loc + 1:]
+
+    cross0 = (cross_sum + m_loc * tdot(dev_both[:, :obs], dev_row)) / (count - 1.0)
+    current1 = state + full_dot(gain0.T, cross0)
+
+    row_mean1 = row_mean0 + full_dot(w0[None, :], cross0)[0]
+    mean1 = mean1 + full_dot(w0[None, :], zp)[0]
+    x1 = x1 + full_dot(gain0.T, zp)
+    gram1 = k1 - tdot(zs, wmat) + 0.25 * tdot(wmat, full_dot(gram0, wmat))
+    anom1 = x1 - mean1[None, :]
+    d1 = obs_values[1] - mean1
+    rhs1 = d1[:, None] - 0.5 * anom1.T
+    gain1 = block_solve(lower_blocks(gram1, size, noise_var[1], count), rhs1, size)
+    cross1_loc = tdot(anom1, current1 - row_mean1[None, :])
+    cross1 = tree_sum(cross1_loc, "member") / (count - 1.0)
+    return current1 + full_dot(gain1.T, cross1)
+
+
+def shards(state, obs_values, noise_var, obs_rows, owner):
+    if obs_rows.shape[0] == 2:
+        return two_blocks(state, obs_values, noise_var, obs_rows, owner)
+    return serial(state, obs_values, noise_var, obs_rows, owner)
+
+
 def solution(mesh):
     placed = (P("member", "state"), P(), P(), P(), P())
     return jax.shard_map(

time: 352 us -> 393 us (1.12)
  local copies, waits for them, and re-layouts: 27.3 us -> 56.1 us
  matrix products: 22.5 us -> 50.9 us
  other arithmetic: 139 us -> 163 us
  waiting for transfers between devices: 99.1 us -> 78.4 us
  starting transfers between devices: 56.6 us -> 37.2 us
    unnamed x21 -> x116, local copies, waits for them, and re-layouts: 3.78 us -> 28 us
    ppermute x24 -> x12, waiting for transfers between devices: 52.8 us -> 34.7 us  [tree_sum(): cur = keep + lax.ppermute(away, axis, perm)]
    dot_general x29 -> x32, matrix products: 10.6 us -> 28.1 us  [full_dot(): jnp.dot(left, right, precision=lax.Precision.HIGHEST, preferred_element_t...]
    dynamic_update_slice x32 -> x1, local copies, waits for them, and re-layouts: 15.3 us -> 0.61 us  [two_blocks(): lax.dynamic_update_slice(slots, jnp.concatenate([both_loc, row_loc])[None...]
    ppermute x24 -> x12, starting transfers between devices: 25.8 us -> 15.3 us  [tree_sum(): other = lax.ppermute(cur, axis, perm)]
    dot_general x20 -> x19, matrix products: 10.2 us -> 20.2 us  [tdot(): lax.dot_general(left, right, (((0,), (0,)), ((), ())), precision=lax.Prec...]
    ppermute x24 -> x12, starting transfers between devices: 26.3 us -> 18.9 us  [tree_sum(): cur = keep + lax.ppermute(away, axis, perm)]
    add x10 -> x15, other arithmetic: 0.65 us -> 7.35 us  [the longest x12 4.15 us: tree_sum(): cur = keep + lax.ppermute(away, axis, perm)]
  transfers between devices with their start and end apart: 50 -> 25, of which waited for: 30 -> 21; matrix products, arithmetic and copies ran while one was open for 5% -> 11% of each run, Pallas kernels for 0% -> 0%
where the time goes in v1:
time: 393 us; the launch traced here: 387 us
  other arithmetic  163 us (41%)
  waiting for transfers between devices  78.4 us (20%)
  local copies, waits for them, and re-layouts  56.1 us (14%)
  matrix products  50.9 us (13%)
  starting transfers between devices  37.2 us (9%)
    another operation x19, other arithmetic, block_solve(): diag = lax.linalg.cholesky(blk[k][k], symmetrize_input=False)  79.4 us
    another operation x12, other arithmetic, block_solve(): inv[k] = lax.linalg.triangular_solve(diag, eye, left_side=True, lower=True)  67.1 us
    ppermute x12, waiting for transfers between devices, tree_sum(): cur = keep + lax.ppermute(away, axis, perm)  34.7 us
    ppermute x12, waiting for transfers between devices, tree_sum(): other = lax.ppermute(cur, axis, perm)  34.6 us
    dot_general x32, matrix products, full_dot(): jnp.dot(left, right, precision=lax.Precision.HIGHEST, preferred_element_t...  28.1 us
    unnamed x116, local copies, waits for them, and re-layouts  28 us
    dot_general x19, matrix products, tdot(): lax.dot_general(left, right, (((0,), (0,)), ((), ())), precision=lax.Prec...  20.2 us
    ppermute x12, starting transfers between devices, tree_sum(): cur = keep + lax.ppermute(away, axis, perm)  18.9 us
  transfers between devices with their start and end apart: 25, of which 21 were waited for; matrix products, arithmetic and copies ran while one was open for 11% of the time, Pallas kernels for 0%

profile of v1, /device:TPU:0, one launch (start us, length us, event | category | flops | bytes accessed | tf_op | source)
XLA Modules:
  0.0 387.5 jit_solution(14074492206737920512)
XLA Ops:
  4.7 3.0 collective-permute-start
  7.8 9.0 %collective-permute-done = f32[128,768]{1,0:T(8,128)S(1)} collective-permute-done((f32[128,768]{1,0:T(8,128)S(1)}, f32[128,768]{1,0:T(8,128)S(1)}, u32[]{:S(2)}, u32[]{:S(2)}) %collective-permute-start) | collective-permute-done | bytes 393248 | tf_op jit(solution)/shard_map/ppermute | solution.py:56
  30.9 9.4 %collective-permute-done.2 = f32[716,128]{0,1:T(8,128)S(1)} collective-permute-done((f32[716,128]{0,1:T(8,128)S(1)}, f32[716,128]{0,1:T(8,128)S(1)}, u32[]{:S(2)}, u32[]{:S(2)}) %collective-permute-start.2) | collective-permute-done | bytes 366624 | tf_op jit(solution)/shard_map/ppermute | solution.py:37
  42.4 4.3 %collective-permute-done.3 = f32[358,128]{0,1:T(8,128)S(1)} collective-permute-done((f32[358,128]{0,1:T(8,128)S(1)}, f32[358,128]{0,1:T(8,128)S(1)}, u32[]{:S(2)}, u32[]{:S(2)}) %collective-permute-start.3) | collective-permute-done | bytes 183328 | tf_op jit(solution)/shard_map/ppermute | solution.py:37
  47.0 2.8 collective-permute-start.4
  49.8 4.9 %collective-permute-done.4 = f32[179,128]{0,1:T(8,128)S(1)} collective-permute-done((f32[179,128]{0,1:T(8,128)S(1)}, f32[179,128]{0,1:T(8,128)S(1)}, u32[]{:S(2)}, u32[]{:S(2)}) %collective-permute-start.4) | collective-permute-done | bytes 91680 | tf_op jit(solution)/shard_map/ppermute | solution.py:37
  55.9 5.0 %collective-permute-done.5 = f32[179,128]{0,1:T(8,128)S(1)} collective-permute-done((f32[179,128]{0,1:T(8,128)S(1)}, f32[179,128]{0,1:T(8,128)S(1)}, u32[]{:S(2)}, u32[]{:S(2)}) %collective-permute-start.5) | collective-permute-done | bytes 91680 | tf_op jit(solution)/shard_map/ppermute | solution.py:43
  63.5 3.6 collective-permute-done.6
  68.9 6.3 %collective-permute-done.7 = f32[716,128]{0,1:T(8,128)S(1)} collective-permute-done((f32[716,128]{0,1:T(8,128)S(1)}, f32[716,128]{0,1:T(8,128)S(1)}, u32[]{:S(2)}, u32[]{:S(2)}) %collective-permute-start.7) | collective-permute-done | bytes 366624 | tf_op jit(solution)/shard_map/ppermute | solution.py:43
  111.2 3.8 multiply_add_fusion
  116.7 11.9 %custom-call.16 = f32[128,128]{1,0:T(8,128)S(1)} custom-call(f32[128,128]{1,0:T(8,128)S(1)} %copy.195), custom_call_target="Cholesky" | custom-call | tf_op jit(solution)/shard_map/cholesky/custom-call.1 | solution.py:69
  130.0 9.8 %custom-call.17 = f32[1,128,128]{1,2,0:T(8,128)S(1)} custom-call(f32[1,128,128]{2,1,0:T(8,128)S(1)} %fusion.48), custom_call_target="InvertDiagBlocksLowerTriangular" | custom-call | tf_op jit(solution)/shard_map/triangular_solve/custom-call.0 | solution.py:70
  147.3 11.7 %custom-call.18 = f32[128,128]{1,0:T(8,128)S(1)} custom-call(f32[128,128]{1,0:T(8,128)S(1)} %copy.201), custom_call_target="Cholesky" | custom-call | tf_op jit(solution)/shard_map/cholesky/custom-call.1 | solution.py:69
  160.4 9.8 %custom-call.19 = f32[1,128,128]{1,2,0:T(8,128)S(1)} custom-call(f32[1,128,128]{2,1,0:T(8,128)S(1)} %fusion.49), custom_call_target="InvertDiagBlocksLowerTriangular" | custom-call | tf_op jit(solution)/shard_map/triangular_solve/custom-call.0 | solution.py:70
  174.8 11.7 %custom-call.20 = f32[128,128]{1,0:T(8,128)S(1)} custom-call(f32[128,128]{1,0:T(8,128)S(1)} %copy.209), custom_call_target="Cholesky" | custom-call | tf_op jit(solution)/shard_map/cholesky/custom-call.1 | solution.py:69
  187.7 9.8 %custom-call.21 = f32[1,128,128]{1,2,0:T(8,128)S(1)} custom-call(f32[1,128,128]{2,1,0:T(8,128)S(1)} %fusion.50), custom_call_target="InvertDiagBlocksLowerTriangular" | custom-call | tf_op jit(solution)/shard_map/triangular_solve/custom-call.0 | solution.py:70
  205.2 2.5 fusion.10
  219.2 12.5 %custom-call.22 = f32[128,128]{1,0:T(8,128)S(1)} custom-call(f32[128,128]{1,0:T(8,128)} %fusion.64), custom_call_target="Cholesky" | custom-call | tf_op jit(solution)/shard_map/cholesky/custom-call.1 | solution.py:69
  233.8 10.6 %custom-call.23 = f32[1,128,128]{1,2,0:T(8,128)S(1)} custom-call(f32[1,128,128]{2,1,0:T(8,128)} %fusion.51), custom_call_target="InvertDiagBlocksLowerTriangular" | custom-call | tf_op jit(solution)/shard_map/triangular_solve/custom-call.0 | solution.py:70
  249.8 13.3 %custom-call.24 = f32[128,128]{1,0:T(8,128)} custom-call(f32[128,128]{1,0:T(8,128)} %convolution_subtract_fusion.16), custom_call_target="Cholesky" | custom-call | tf_op jit(solution)/shard_map/cholesky/custom-call.1 | solution.py:69
  266.9 11.3 %custom-call.25 = f32[1,128,128]{1,2,0:T(8,128)} custom-call(f32[1,128,128]{2,1,0:T(8,128)} %fusion.52), custom_call_target="InvertDiagBlocksLowerTriangular" | custom-call | tf_op jit(solution)/shard_map/triangular_solve/custom-call.0 | solution.py:70
  291.7 3.0 collective-permute-done.10
  300.8 3.1 collective-permute-start.12
  306.1 3.0 collective-permute-start.13
  315.3 13.2 %custom-call.26 = f32[128,128]{1,0:T(8,128)} custom-call(f32[128,128]{1,0:T(8,128)} %convolution_subtract_fusion.12), custom_call_target="Cholesky" | custom-call | tf_op jit(solution)/shard_map/cholesky/custom-call.1 | solution.py:69
  332.2 3.7 collective-permute-done.15
  345.9 9.8 %custom-call.27 = f32[1,128,128]{1,2,0:T(8,128)S(1)} custom-call(f32[1,128,128]{2,1,0:T(8,128)S(1)} %fusion.53), custom_call_target="InvertDiagBlocksLowerTriangular" | custom-call | tf_op jit(solution)/shard_map/triangular_solve/custom-call.0 | solution.py:70
  356.5 4.8 %collective-permute-done.19 = f32[48,640]{1,0:T(8,128)S(1)} collective-permute-done((f32[48,640]{1,0:T(8,128)S(1)}, f32[48,640]{1,0:T(8,128)S(1)}, u32[]{:S(2)}, u32[]{:S(2)}) %collective-permute-start.19) | collective-permute-done | bytes 122912 | tf_op jit(solution)/shard_map/ppermute | solution.py:37
  361.3 3.2 collective-permute-start.20
  367.1 2.6 collective-permute-start.21
  372.8 4.6 %collective-permute-done.22 = f32[48,640]{1,0:T(8,128)S(1)} collective-permute-done((f32[48,640]{1,0:T(8,128)S(1)}, f32[48,640]{1,0:T(8,128)S(1)}, u32[]{:S(2)}, u32[]{:S(2)}) %collective-permute-start.22) | collective-permute-done | bytes 122912 | tf_op jit(solution)/shard_map/ppermute | solution.py:43
  378.5 5.1 %collective-permute-done.23 = f32[96,640]{1,0:T(8,128)S(1)} collective-permute-done((f32[96,640]{1,0:T(8,128)S(1)}, f32[96,640]{1,0:T(8,128)S(1)}, u32[]{:S(2)}, u32[]{:S(2)}) %collective-permute-start.23) | collective-permute-done | bytes 245792 | tf_op jit(solution)/shard_map/ppermute | solution.py:43
  (340 shorter events, 162.3 us)
Async XLA Ops:
  4.7 12.1 %collective-permute-start = (f32[128,768]{1,0:T(8,128)S(1)}, f32[128,768]{1,0:T(8,128)S(1)}, u32[]{:S(2)}, u32[]{:S(2)}) collective-permute-start(f32[128,768]{1,0:T(8,128)S(1)} %maximum_select_fusion.6), channel_id=1, source_target_pairs={{0,16},{16,0},{1,17},{17,1},{2,18},{18,2},{3,19},{19,3},{4,20},{20... | collective-permute-start | bytes 1179656 | tf_op jit(solution)/shard_map/ppermute | solution.py:56
  16.9 123.8 %copy-start.1 = (f32[128,768]{1,0:T(8,128)}, f32[128,768]{1,0:T(8,128)S(1)}, u32[]{:S(2)}) copy-start(f32[128,768]{1,0:T(8,128)S(1)} %get-tuple-element.21) | copy-start | bytes 1179652
  23.6 2.4 collective-permute-start.1
  29.0 11.2 %collective-permute-start.2 = (f32[716,128]{0,1:T(8,128)S(1)}, f32[716,128]{0,1:T(8,128)S(1)}, u32[]{:S(2)}, u32[]{:S(2)}) collective-permute-start(f32[716,128]{0,1:T(8,128)S(1)} %constant_dynamic-slice_fusion.10), channel_id=1, source_target_pairs={{0,2},{1,3},{2,0},{3,1},{4,6},{5,7},{6,4},{7,5},{8,10},{9,11},{10,... | collective-permute-start | bytes 1099784 | tf_op jit(solution)/shard_map/ppermute | solution.py:37
  40.5 6.2 %collective-permute-start.3 = (f32[358,128]{0,1:T(8,128)S(1)}, f32[358,128]{0,1:T(8,128)S(1)}, u32[]{:S(2)}, u32[]{:S(2)}) collective-permute-start(f32[358,128]{0,1:T(8,128)S(1)} %constant_dynamic-slice_fusion.9), channel_id=1, source_target_pairs={{0,4},{1,5},{2,6},{3,7},{4,0},{5,1},{6,2},{7,3},{8,12},{9,13},{10,... | collective-permute-start | bytes 549896 | tf_op jit(solution)/shard_map/ppermute | solution.py:37
  47.0 7.7 %collective-permute-start.4 = (f32[179,128]{0,1:T(8,128)S(1)}, f32[179,128]{0,1:T(8,128)S(1)}, u32[]{:S(2)}, u32[]{:S(2)}) collective-permute-start(f32[179,128]{0,1:T(8,128)S(1)} %constant_dynamic-slice_fusion.8), channel_id=1, source_target_pairs={{0,8},{1,9},{2,10},{3,11},{4,12},{5,13},{6,14},{7,15},{8,0},{9,1},... | collective-permute-start | bytes 274952 | tf_op jit(solution)/shard_map/ppermute | solution.py:37
  49.8 27.1 %copy-start.30 = (f32[2,384]{1,0:T(2,128)S(1)}, f32[2,384]{1,0:T(2,128)}, u32[]{:S(2)}) copy-start(f32[2,384]{1,0:T(2,128)} %param.11) | copy-start | bytes 9220
  49.8 27.7 %copy-start.31 = (f32[2,384]{1,0:T(2,128)S(1)}, f32[2,384]{1,0:T(2,128)}, u32[]{:S(2)}) copy-start(f32[2,384]{1,0:T(2,128)} %param.12) | copy-start | bytes 9220
  54.8 6.1 %collective-permute-start.5 = (f32[179,128]{0,1:T(8,128)S(1)}, f32[179,128]{0,1:T(8,128)S(1)}, u32[]{:S(2)}, u32[]{:S(2)}) collective-permute-start(f32[179,128]{0,1:T(8,128)S(1)} %dynamic-slice_add_fusion.7), channel_id=1, source_target_pairs={{0,8},{1,9},{2,10},{3,11},{4,12},{5,13},{6,14},{7,15},{8,0},{9,1},... | collective-permute-start | bytes 274952 | tf_op jit(solution)/shard_map/ppermute | solution.py:43
  61.0 6.1 %collective-permute-start.6 = (f32[358,128]{0,1:T(8,128)S(1)}, f32[358,128]{0,1:T(8,128)S(1)}, u32[]{:S(2)}, u32[]{:S(2)}) collective-permute-start(f32[358,128]{0,1:T(8,128)S(1)} %maximum_select_fusion.10), channel_id=1, source_target_pairs={{0,4},{1,5},{2,6},{3,7},{4,0},{5,1},{6,2},{7,3},{8,12},{9,13},{10,... | collective-permute-start | bytes 549896 | tf_op jit(solution)/shard_map/ppermute | solution.py:43
  67.4 7.8 %collective-permute-start.7 = (f32[716,128]{0,1:T(8,128)S(1)}, f32[716,128]{0,1:T(8,128)S(1)}, u32[]{:S(2)}, u32[]{:S(2)}) collective-permute-start(f32[716,128]{0,1:T(8,128)S(1)} %maximum_select_fusion.7), channel_id=1, source_target_pairs={{0,2},{1,3},{2,0},{3,1},{4,6},{5,7},{6,4},{7,5},{8,10},{9,11},{10,... | collective-permute-start | bytes 1099784 | tf_op jit(solution)/shard_map/ppermute | solution.py:43
  76.7 3.4 collective-permute-start.8
  76.8 39.2 %copy-start.22 = (pred[128,128]{0,1:T(32,128)(4,1)}, pred[128,128]{0,1:T(32,128)(4,1)S(1)}, u32[]{:S(2)}) copy-start(pred[128,128]{0,1:T(32,128)(4,1)S(1)} %copy.193) | copy-start | bytes 49156
  111.2 29.5 %copy-start.25 = (f32[1408]{0:T(1024)}, f32[1408]{0:T(1024)S(1)}, u32[]{:S(2)}) copy-start(f32[1408]{0:T(1024)S(1)} %broadcast_multiply_fusion) | copy-start | bytes 16900
  172.5 26.9 %copy-start.14 = (f32[128,128]{1,0:T(8,128)}, f32[128,128]{1,0:T(8,128)S(1)}, u32[]{:S(2)}) copy-start(f32[128,128]{1,0:T(8,128)S(1)} %fusion.101) | copy-start | bytes 196612
  279.3 4.7 %collective-permute-start.9 = (f32[192,640]{1,0:T(8,128)S(1)}, f32[192,640]{1,0:T(8,128)S(1)}, u32[]{:S(2)}, u32[]{:S(2)}) collective-permute-start(f32[192,640]{1,0:T(8,128)S(1)} %constant_dynamic-slice_fusion.7), channel_id=1, source_target_pairs={{0,1},{1,0},{2,3},{3,2},{4,5},{5,4},{6,7},{7,6},{8,9},{9,8},{10,11... | collective-permute-start | bytes 1474568 | tf_op jit(solution)/shard_map/ppermute | solution.py:37
  286.5 8.2 %collective-permute-start.10 = (f32[96,640]{1,0:T(8,128)}, f32[96,640]{1,0:T(8,128)}, u32[]{:S(2)}, u32[]{:S(2)}) collective-permute-start(f32[96,640]{1,0:T(8,128)} %constant_dynamic-slice_fusion.6), channel_id=1, source_target_pairs={{0,2},{1,3},{2,0},{3,1},{4,6},{5,7},{6,4},{7,5},{8,10},{9,11},{10,... | collective-permute-start | bytes 737288 | tf_op jit(solution)/shard_map/ppermute | solution.py:37
  295.8 4.9 %collective-permute-start.11 = (f32[48,640]{1,0:T(8,128)S(1)}, f32[48,640]{1,0:T(8,128)S(1)}, u32[]{:S(2)}, u32[]{:S(2)}) collective-permute-start(f32[48,640]{1,0:T(8,128)S(1)} %constant_dynamic-slice_fusion.5), channel_id=1, source_target_pairs={{0,4},{1,5},{2,6},{3,7},{4,0},{5,1},{6,2},{7,3},{8,12},{9,13},{10,... | collective-permute-start | bytes 368648 | tf_op jit(solution)/shard_map/ppermute | solution.py:37
  300.8 5.3 %collective-permute-start.12 = (f32[24,640]{1,0:T(8,128)S(1)}, f32[24,640]{1,0:T(8,128)S(1)}, u32[]{:S(2)}, u32[]{:S(2)}) collective-permute-start(f32[24,640]{1,0:T(8,128)S(1)} %constant_dynamic-slice_fusion.4), channel_id=1, source_target_pairs={{0,8},{1,9},{2,10},{3,11},{4,12},{5,13},{6,14},{7,15},{8,0},{9,1},... | collective-permute-start | bytes 184328 | tf_op jit(solution)/shard_map/ppermute | solution.py:37
  306.1 5.2 %collective-permute-start.13 = (f32[24,640]{1,0:T(8,128)S(1)}, f32[24,640]{1,0:T(8,128)S(1)}, u32[]{:S(2)}, u32[]{:S(2)}) collective-permute-start(f32[24,640]{1,0:T(8,128)S(1)} %dynamic-slice_add_fusion.11), channel_id=1, source_target_pairs={{0,8},{1,9},{2,10},{3,11},{4,12},{5,13},{6,14},{7,15},{8,0},{9,1},... | collective-permute-start | bytes 184328 | tf_op jit(solution)/shard_map/ppermute | solution.py:43
  311.9 16.6 %collective-permute-start.14 = (f32[48,640]{1,0:T(8,128)}, f32[48,640]{1,0:T(8,128)}, u32[]{:S(2)}, u32[]{:S(2)}) collective-permute-start(f32[48,640]{1,0:T(8,128)} %maximum_select_fusion.11), channel_id=1, source_target_pairs={{0,4},{1,5},{2,6},{3,7},{4,0},{5,1},{6,2},{7,3},{8,12},{9,13},{10,... | collective-permute-start | bytes 368648 | tf_op jit(solution)/shard_map/ppermute | solution.py:43
  329.7 6.3 %collective-permute-start.15 = (f32[96,640]{1,0:T(8,128)S(1)}, f32[96,640]{1,0:T(8,128)S(1)}, u32[]{:S(2)}, u32[]{:S(2)}) collective-permute-start(f32[96,640]{1,0:T(8,128)S(1)} %maximum_select_fusion.8), channel_id=1, source_target_pairs={{0,2},{1,3},{2,0},{3,1},{4,6},{5,7},{6,4},{7,5},{8,10},{9,11},{10,... | collective-permute-start | bytes 737288 | tf_op jit(solution)/shard_map/ppermute | solution.py:43
  336.0 1.9 collective-permute-start.16
  341.7 1.9 collective-permute-start.17
  343.7 12.4 %collective-permute-start.18 = (f32[96,640]{1,0:T(8,128)S(1)}, f32[96,640]{1,0:T(8,128)S(1)}, u32[]{:S(2)}, u32[]{:S(2)}) collective-permute-start(f32[96,640]{1,0:T(8,128)S(1)} %constant_dynamic-slice_fusion.2), channel_id=1, source_target_pairs={{0,2},{1,3},{2,0},{3,1},{4,6},{5,7},{6,4},{7,5},{8,10},{9,11},{10,... | collective-permute-start | bytes 737288 | tf_op jit(solution)/shard_map/ppermute | solution.py:37
  356.1 28.2 %copy-start.10 = (f32[128,128]{1,0:T(8,128)S(1)}, f32[128,128]{1,0:T(8,128)}, u32[]{:S(2)}) copy-start(f32[128,128]{1,0:T(8,128)} %copy-done.8) | copy-start | bytes 196612
  356.1 5.2 %collective-permute-start.19 = (f32[48,640]{1,0:T(8,128)S(1)}, f32[48,640]{1,0:T(8,128)S(1)}, u32[]{:S(2)}, u32[]{:S(2)}) collective-permute-start(f32[48,640]{1,0:T(8,128)S(1)} %constant_dynamic-slice_fusion.1), channel_id=1, source_target_pairs={{0,4},{1,5},{2,6},{3,7},{4,0},{5,1},{6,2},{7,3},{8,12},{9,13},{10,... | collective-permute-start | bytes 368648 | tf_op jit(solution)/shard_map/ppermute | solution.py:37
  361.3 5.8 %collective-permute-start.20 = (f32[24,640]{1,0:T(8,128)S(1)}, f32[24,640]{1,0:T(8,128)S(1)}, u32[]{:S(2)}, u32[]{:S(2)}) collective-permute-start(f32[24,640]{1,0:T(8,128)S(1)} %constant_dynamic-slice_fusion), channel_id=1, source_target_pairs={{0,8},{1,9},{2,10},{3,11},{4,12},{5,13},{6,14},{7,15},{8,0},{9,1},... | collective-permute-start | bytes 184328 | tf_op jit(solution)/shard_map/ppermute | solution.py:37
  367.1 5.2 %collective-permute-start.21 = (f32[24,640]{1,0:T(8,128)S(1)}, f32[24,640]{1,0:T(8,128)S(1)}, u32[]{:S(2)}, u32[]{:S(2)}) collective-permute-start(f32[24,640]{1,0:T(8,128)S(1)} %dynamic-slice_add_fusion.10), channel_id=1, source_target_pairs={{0,8},{1,9},{2,10},{3,11},{4,12},{5,13},{6,14},{7,15},{8,0},{9,1},... | collective-permute-start | bytes 184328 | tf_op jit(solution)/shard_map/ppermute | solution.py:43
  372.4 4.9 %collective-permute-start.22 = (f32[48,640]{1,0:T(8,128)S(1)}, f32[48,640]{1,0:T(8,128)S(1)}, u32[]{:S(2)}, u32[]{:S(2)}) collective-permute-start(f32[48,640]{1,0:T(8,128)S(1)} %maximum_select_fusion.12), channel_id=1, source_target_pairs={{0,4},{1,5},{2,6},{3,7},{4,0},{5,1},{6,2},{7,3},{8,12},{9,13},{10,... | collective-permute-start | bytes 368648 | tf_op jit(solution)/shard_map/ppermute | solution.py:43
  377.4 6.3 %collective-permute-start.23 = (f32[96,640]{1,0:T(8,128)S(1)}, f32[96,640]{1,0:T(8,128)S(1)}, u32[]{:S(2)}, u32[]{:S(2)}) collective-permute-start(f32[96,640]{1,0:T(8,128)S(1)} %maximum_select_fusion.9), channel_id=1, source_target_pairs={{0,2},{1,3},{2,0},{3,1},{4,6},{5,7},{6,4},{7,5},{8,10},{9,11},{10,... | collective-permute-start | bytes 737288 | tf_op jit(solution)/shard_map/ppermute | solution.py:43
  383.7 1.9 collective-permute-start.24
  (27 other events, 158.9 us)
